TPU v7x, 512 devices: a whole 4x4x16 slice. The times are simulated.
512 devices in a mesh: segment: 8 (over y_hi, x), dp: 64 (over y_lo, z, core).
Axes of the slice: x: 4, y: 4 (y_hi: 2, y_lo: 2; y = y_hi * 2 + y_lo), z: 16, core: 2. Of those that a mesh axis runs over, the one named last changes fastest.
Arguments:
- acts: bfloat16 [8, 128, 4, 8, 8, 128], P('segment', 'dp'), may hold values from -6 to 6
- weights: bfloat16 [8, 3456, 128], P('segment', 'dp'), may hold values from -0.109375 to 0.109375
- pos_weight: float32 [8, 3, 128], P('segment'), may hold values from -4 to 4
- anchors: int32 [128, 3], P('dp'), may hold values from 0 to 1983
- top_grad: bfloat16 [128, 4, 8, 8, 128], P('dp'), may hold values from -6 to 6
Outputs:
- section_grads: bfloat16 [8, 128, 4, 8, 8, 128], P('segment', 'dp')
- weight_grad: float32 [8, 3456, 128], P('segment', 'dp')
Inputs may be any that keep to these rules, and one draw needn't show every extreme that they name: `anchors`: mesh coordinates of each crop's corner.
All inputs are finite; a program needn't handle non-finite values.
Results may differ from a plain program's by a relative error of at most 0.015.
Values may be sent and summed in bfloat16 or wider, within the bound.
No kernel may reach another device: no remote copies, remote signals or barrier semaphores. Data moves between devices by JAX's collectives and lax.ppermute only.
A program may use at most 64 MiB of HBM per device.

v0:
```python
import math
import jax
import jax.numpy as jnp
from jax import lax
from jax.sharding import PartitionSpec as P

STRIDE = 2
WAVE = 64


def passed_along(array, axis, by):
    length = lax.axis_size(axis)
    pairs = [(i, i + by) for i in range(length) if 0 <= i + by < length]
    return lax.ppermute(array, axis, pairs)


def apply_taps(field, kernel_taps):
    size_x, size_y, size_z, channels = field.shape
    padded = jnp.pad(field, ((1, 1), (1, 1), (1, 1), (0, 0)))
    summed = jnp.zeros((size_x * size_y * size_z, kernel_taps.shape[2]), jnp.float32)
    tap_index = 0
    for first in range(3):
        for second in range(3):
            for third in range(3):
                window_rows = padded[
                    first : first + size_x, second : second + size_y, third : third + size_z
                ].reshape(size_x * size_y * size_z, channels)
                summed = summed + jnp.dot(
                    window_rows, kernel_taps[tap_index], preferred_element_type=jnp.float32
                )
                tap_index += 1
    return summed


def tap_grads(field, slope):
    size_x, size_y, size_z, channels = field.shape
    padded = jnp.pad(field, ((1, 1), (1, 1), (1, 1), (0, 0)))
    blocks = []
    for first in range(3):
        for second in range(3):
            for third in range(3):
                window_rows = padded[
                    first : first + size_x, second : second + size_y, third : third + size_z
                ].reshape(size_x * size_y * size_z, channels)
                blocks.append(jnp.dot(window_rows.T, slope, preferred_element_type=jnp.float32))
    return jnp.concatenate(blocks, axis=0)


def position_term(anchor, pos_gain, size_x, size_y, size_z):
    phases = []
    for axis_num, axis_len in enumerate((size_x, size_y, size_z)):
        coords = anchor[axis_num] + STRIDE * jnp.arange(axis_len, dtype=jnp.int32)
        phase_val = (coords % WAVE).astype(jnp.float32)
        phases.append(jnp.sin(phase_val * (2.0 * math.pi / WAVE)))
    position_sum = (
        phases[0][:, None, None, None] * pos_gain[0]
        + phases[1][None, :, None, None] * pos_gain[1]
        + phases[2][None, None, :, None] * pos_gain[2]
    )
    return position_sum.reshape(size_x * size_y * size_z, pos_gain.shape[1])


def layer_slope(incoming_rows, pre_act):
    sigmoid_h = jax.nn.sigmoid(pre_act)
    silu_slope = sigmoid_h * (1.0 + pre_act * (1.0 - sigmoid_h))
    return (incoming_rows * silu_slope).astype(jnp.bfloat16)


def local(acts, weights, pos_weight, anchors, top_grad):
    segments = lax.axis_size("segment")
    dp_count = lax.axis_size("dp")
    segment_index = lax.axis_index("segment")
    gathered = lax.all_gather(weights[0], "dp", axis=0, tiled=True)
    channels = gathered.shape[1]
    kernel_taps = gathered.reshape(-1, channels, channels)
    flipped = jnp.transpose(jnp.flip(kernel_taps, 0), (0, 2, 1))
    inputs_local = acts[0]
    micro_count = inputs_local.shape[0]
    size_x, size_y, size_z = (inputs_local.shape[1], inputs_local.shape[2], inputs_local.shape[3])
    cell_count = size_x * size_y * size_z
    rows_local = weights.shape[1]
    pos_gain = pos_weight[0]
    position_all = jnp.stack(
        [
            position_term(anchors[micro], pos_gain, size_x, size_y, size_z)
            for micro in range(micro_count)
        ]
    )
    tick_count = segments + micro_count - 1
    scale_factor = 1.0 / math.sqrt(dp_count * micro_count * cell_count)

    def tick_step(step_num, carry):
        incoming, grads_held, slopes_held, accumulated = carry
        micro_index = step_num - (segments - 1 - segment_index)
        active = (micro_index >= 0) & (micro_index < micro_count)
        slot_index = jnp.clip(micro_index, 0, micro_count - 1)

        def busy_work(operands):
            incoming_in, grads_in, slopes_in = operands
            top_slice = lax.dynamic_index_in_dim(top_grad, slot_index, 0, keepdims=False)
            cotangent = jnp.where(segment_index == segments - 1, top_slice, incoming_in)
            field = lax.dynamic_index_in_dim(inputs_local, slot_index, 0, keepdims=False)
            pre_act = apply_taps(field, kernel_taps) + lax.dynamic_index_in_dim(
                position_all, slot_index, 0, keepdims=False
            )
            incoming_rows = cotangent.reshape(cell_count, channels).astype(jnp.float32)
            slope = layer_slope(incoming_rows, pre_act)
            down_grad = (
                incoming_rows + apply_taps(slope.reshape(size_x, size_y, size_z, channels), flipped)
            ).astype(jnp.bfloat16)
            down_grad = down_grad.reshape(size_x, size_y, size_z, channels)
            grads_out = lax.dynamic_update_index_in_dim(grads_in, down_grad, slot_index, 0)
            slopes_out = lax.dynamic_update_index_in_dim(slopes_in, slope, slot_index, 0)
            grad_term = jnp.zeros((1, channels), jnp.float32)
            return (down_grad, grads_out, slopes_out, grad_term)

        def quiet_work(operands):
            incoming_in, grads_in, slopes_in = operands
            grad_term = jnp.zeros((1, channels), jnp.float32)
            return (jnp.zeros_like(incoming_in), grads_in, slopes_in, grad_term)

        down_grad, grads_held, slopes_held, grad_term = lax.cond(
            active, busy_work, quiet_work, (incoming, grads_held, slopes_held)
        )
        incoming = passed_along(down_grad, "segment", -1)
        return (incoming, grads_held, slopes_held, accumulated)

    start_carry = (
        jnp.zeros((size_x, size_y, size_z, channels), jnp.bfloat16),
        jnp.zeros(inputs_local.shape, jnp.bfloat16),
        jnp.zeros((micro_count, cell_count, channels), jnp.bfloat16),
        jnp.zeros((rows_local, channels), jnp.float32),
    )
    incoming, grads_held, slopes_held, accumulated = lax.fori_loop(
        0, tick_count, tick_step, start_carry
    )
    grad_term = tap_grads(inputs_local[0], slopes_held[0])
    micro = 1
    grad_term = grad_term + tap_grads(inputs_local[micro], slopes_held[micro])
    reduced = lax.psum_scatter(grad_term, "dp", scatter_dimension=0, tiled=True)
    return (grads_held[None], (reduced * scale_factor)[None])


def solution(mesh):
    return jax.shard_map(
        local,
        mesh=mesh,
        in_specs=(
            P("segment", "dp", None, None, None, None),
            P("segment", "dp", None),
            P("segment", None, None),
            P("dp", None),
            P("dp", None, None, None, None),
        ),
        out_specs=(P("segment", "dp", None, None, None, None), P("segment", "dp", None)),
        check_vma=False,
    )
```

profile of v0, /device:TPU:1, one launch (start us, length us, event | category | flops | bytes accessed | tf_op | source)
XLA Modules:
  0.0 428.4 jit_solution(7778404728182434695)
XLA Ops:
  0.6 1.6 fusion.250
  5.3 75.9 %all-gather = bf16[1,3456,128]{2,0,1:T(2,128)(2,1)S(1)} all-gather(bf16[1,54,128]{2,0,1:T(2,128)(2,1)S(1)} %copy.12), channel_id=2, replica_groups=mesh['segment'=8,'dp'=64] {'dp'}, dimensions={1}, use_global_device_ids=true | all-gather | bytes 898560 | tf_op jit(solution)/shard_map/all_gather | solution.py:73
  89.9 157.1 %while.18 = (s32[]{:T(128)}, bf16[4,8,8,128]{3,2,1,0:T(8,128)(2,1)S(1)}, bf16[2,4,8,8,128]{4,3,2,1,0:T(8,128)(2,1)}, bf16[2,256,128]{2,1,0:T(8,128)(2,1)S(1)}, s...) while((s32[]{:T(128)}, ...), condition=%wide.region_3.4_spmd, body=%wide.region_0.3_spmd.sunk | while | flops 455180288 | bytes 23921024 | solution.py:134
  91.9 4.3 %collective-permute-done = bf16[4,8,8,128]{3,2,1,0:T(8,128)(2,1)S(1)} collective-permute-done((bf16[4,8,8,128]{3,2,1,0:T(8,128)(2,1)}, bf16[4,8,8,128]{3,2,1,0:T(8,128)(2,1)S(1)}, u32[]{:S(2)}, u32[]{:S(2)}) %collective-permute-start) | collective-permute-done | bytes 65568 | tf_op jit(solution)/shard_map/while/body/eval_jaxpr/ppermute | solution.py:14
  98.2 3.9 collective-permute-done
  104.1 3.9 collective-permute-done
  109.9 6.5 %collective-permute-done = bf16[4,8,8,128]{3,2,1,0:T(8,128)(2,1)S(1)} collective-permute-done((bf16[4,8,8,128]{3,2,1,0:T(8,128)(2,1)}, bf16[4,8,8,128]{3,2,1,0:T(8,128)(2,1)S(1)}, u32[]{:S(2)}, u32[]{:S(2)}) %collective-permute-start) | collective-permute-done | bytes 65568 | tf_op jit(solution)/shard_map/while/body/eval_jaxpr/ppermute | solution.py:14
  118.4 7.5 %collective-permute-done = bf16[4,8,8,128]{3,2,1,0:T(8,128)(2,1)S(1)} collective-permute-done((bf16[4,8,8,128]{3,2,1,0:T(8,128)(2,1)}, bf16[4,8,8,128]{3,2,1,0:T(8,128)(2,1)S(1)}, u32[]{:S(2)}, u32[]{:S(2)}) %collective-permute-start) | collective-permute-done | bytes 65568 | tf_op jit(solution)/shard_map/while/body/eval_jaxpr/ppermute | solution.py:14
  127.8 7.5 %collective-permute-done = bf16[4,8,8,128]{3,2,1,0:T(8,128)(2,1)S(1)} collective-permute-done((bf16[4,8,8,128]{3,2,1,0:T(8,128)(2,1)}, bf16[4,8,8,128]{3,2,1,0:T(8,128)(2,1)S(1)}, u32[]{:S(2)}, u32[]{:S(2)}) %collective-permute-start) | collective-permute-done | bytes 65568 | tf_op jit(solution)/shard_map/while/body/eval_jaxpr/ppermute | solution.py:14
  137.3 71.9 %collective-permute-done = bf16[4,8,8,128]{3,2,1,0:T(8,128)(2,1)S(1)} collective-permute-done((bf16[4,8,8,128]{3,2,1,0:T(8,128)(2,1)}, bf16[4,8,8,128]{3,2,1,0:T(8,128)(2,1)S(1)}, u32[]{:S(2)}, u32[]{:S(2)}) %collective-permute-start) | collective-permute-done | bytes 65568 | tf_op jit(solution)/shard_map/while/body/eval_jaxpr/ppermute | solution.py:14
  209.2 11.9 %conditional.2 = (bf16[4,8,8,128]{3,2,1,0:T(8,128)(2,1)}, bf16[2,4,8,8,128]{4,3,2,1,0:T(8,128)(2,1)}, bf16[2,256,128]{2,1,0:T(8,128)(2,1)S(1)}) conditional(s32[]{:T(128)} %convert_element_type.107, (bf16[2,4,8,8,128]{4,3,2,1,0:T(8,128)(2,1)}, bf16[2,256,128]{2,1,0:T(8,128)(2,1)S(1)}) %tuple.170, (s32[]{:T(128)}, s32[]{:T(128)}, ...), branch_computations={%region_1.1_spmd, %region_2.2_spmd} | conditional | flops 455180288 | bytes 23658574 | solution.py:122
  219.6 1.5 constant_dynamic-update-slice_fusion
  222.4 7.5 %collective-permute-done = bf16[4,8,8,128]{3,2,1,0:T(8,128)(2,1)S(1)} collective-permute-done((bf16[4,8,8,128]{3,2,1,0:T(8,128)(2,1)}, bf16[4,8,8,128]{3,2,1,0:T(8,128)(2,1)S(1)}, u32[]{:S(2)}, u32[]{:S(2)}) %collective-permute-start) | collective-permute-done | bytes 65568 | tf_op jit(solution)/shard_map/while/body/eval_jaxpr/ppermute | solution.py:14
  229.9 11.9 %conditional.2 = (bf16[4,8,8,128]{3,2,1,0:T(8,128)(2,1)}, bf16[2,4,8,8,128]{4,3,2,1,0:T(8,128)(2,1)}, bf16[2,256,128]{2,1,0:T(8,128)(2,1)S(1)}) conditional(s32[]{:T(128)} %convert_element_type.107, (bf16[2,4,8,8,128]{4,3,2,1,0:T(8,128)(2,1)}, bf16[2,256,128]{2,1,0:T(8,128)(2,1)S(1)}) %tuple.170, (s32[]{:T(128)}, s32[]{:T(128)}, ...), branch_computations={%region_1.1_spmd, %region_2.2_spmd} | conditional | flops 455180288 | bytes 23658574 | solution.py:122
  243.2 3.9 collective-permute-done
  258.7 122.4 %fusion = f32[64,128]{1,0:T(8,128)S(1)} fusion(f32[3456,128]{1,0:T(8,128)S(1)} %add.436), kind=kCustom, calls=%all-reduce-scatter | all-reduce-scatter fusion | flops 524289 | bytes 1804288
  385.0 11.3 %collective-permute-start.6 = (f32[64,128]{1,0:T(8,128)S(1)}, f32[64,128]{1,0:T(8,128)S(1)}, u32[]{:S(2)}, u32[]{:S(2)}) collective-permute-start(f32[64,128]{1,0:T(8,128)S(1)} %fusion), channel_id=1, source_target_pairs={{0,6},{1,7},{2,8},{3,9},{4,10},{5,11},{6,12},{7,13},{8,14},{9,15},... | collective-permute-start | bytes 98312
  396.3 6.0 %collective-permute-start.10 = (f32[54,128]{1,0:T(8,128)S(1)}, f32[54,128]{1,0:T(8,128)S(1)}, u32[]{:S(2)}, u32[]{:S(2)}) collective-permute-start(f32[54,128]{1,0:T(8,128)S(1)} %slice.604), channel_id=1, source_target_pairs={{0,10},{1,11},{2,12},{3,13},{4,14},{5,15},{6,16},{7,17},{8,18},{9,... | collective-permute-start | bytes 82952
  402.2 1.7 collective-permute-done.10
  404.0 2.0 collective-permute-start.5
  406.0 9.6 %collective-permute-start.4 = (f32[64,128]{1,0:T(8,128)S(1)}, f32[64,128]{1,0:T(8,128)S(1)}, u32[]{:S(2)}, u32[]{:S(2)}) collective-permute-start(f32[64,128]{1,0:T(8,128)S(1)} %fusion), channel_id=1, source_target_pairs={{0,4},{1,5},{2,6},{3,7},{4,8},{5,9},{6,10},{7,11},{8,12},{9,13},{1... | collective-permute-start | bytes 98312
  416.9 3.1 collective-permute-start.2
  420.1 4.0 collective-permute-start.1
  426.1 1.7 concatenate.8
  (346 shorter events, 72.0 us)
Async XLA Ops:
  89.9 158.1 %copy-start.42 = (bf16[4,8,8,128]{3,2,1,0:T(8,128)(2,1)S(1)}, bf16[4,8,8,128]{3,2,1,0:T(8,128)(2,1)}, u32[]{:S(2)}) copy-start(bf16[4,8,8,128]{3,2,1,0:T(8,128)(2,1)} %get-tuple-element.394) | copy-start | bytes 196612
  89.9 158.3 %copy-start.41 = (bf16[4,8,8,128]{3,2,1,0:T(8,128)(2,1)S(1)}, bf16[4,8,8,128]{3,2,1,0:T(8,128)(2,1)}, u32[]{:S(2)}) copy-start(bf16[4,8,8,128]{3,2,1,0:T(8,128)(2,1)} %get-tuple-element.395) | copy-start | bytes 196612
  89.9 158.5 %copy-start.40 = (bf16[4,8,8,128]{3,2,1,0:T(8,128)(2,1)S(1)}, bf16[4,8,8,128]{3,2,1,0:T(8,128)(2,1)}, u32[]{:S(2)}) copy-start(bf16[4,8,8,128]{3,2,1,0:T(8,128)(2,1)} %get-tuple-element.396) | copy-start | bytes 196612
  89.9 158.7 %copy-start.39 = (bf16[4,8,8,128]{3,2,1,0:T(8,128)(2,1)S(1)}, bf16[4,8,8,128]{3,2,1,0:T(8,128)(2,1)}, u32[]{:S(2)}) copy-start(bf16[4,8,8,128]{3,2,1,0:T(8,128)(2,1)} %get-tuple-element.397) | copy-start | bytes 196612
  89.9 158.9 %copy-start.38 = (bf16[4,8,8,128]{3,2,1,0:T(8,128)(2,1)S(1)}, bf16[4,8,8,128]{3,2,1,0:T(8,128)(2,1)}, u32[]{:S(2)}) copy-start(bf16[4,8,8,128]{3,2,1,0:T(8,128)(2,1)} %get-tuple-element.398) | copy-start | bytes 196612
  90.6 5.6 %collective-permute-start = (bf16[4,8,8,128]{3,2,1,0:T(8,128)(2,1)}, bf16[4,8,8,128]{3,2,1,0:T(8,128)(2,1)S(1)}, u32[]{:S(2)}, u32[]{:S(2)}) collective-permute-start(bf16[4,8,8,128]{3,2,1,0:T(8,128)(2,1)} %get-tuple-element.513), channel_id=1, source_target_pairs={{64,0},{128,64},{192,128},{256,192},{320,256},{384,320},{448,384},... | collective-permute-start | bytes 196616 | tf_op jit(solution)/shard_map/while/body/eval_jaxpr/ppermute | solution.py:14
  96.9 5.2 %collective-permute-start = (bf16[4,8,8,128]{3,2,1,0:T(8,128)(2,1)}, bf16[4,8,8,128]{3,2,1,0:T(8,128)(2,1)S(1)}, u32[]{:S(2)}, u32[]{:S(2)}) collective-permute-start(bf16[4,8,8,128]{3,2,1,0:T(8,128)(2,1)} %get-tuple-element.513), channel_id=1, source_target_pairs={{64,0},{128,64},{192,128},{256,192},{320,256},{384,320},{448,384},... | collective-permute-start | bytes 196616 | tf_op jit(solution)/shard_map/while/body/eval_jaxpr/ppermute | solution.py:14
  102.8 5.2 %collective-permute-start = (bf16[4,8,8,128]{3,2,1,0:T(8,128)(2,1)}, bf16[4,8,8,128]{3,2,1,0:T(8,128)(2,1)S(1)}, u32[]{:S(2)}, u32[]{:S(2)}) collective-permute-start(bf16[4,8,8,128]{3,2,1,0:T(8,128)(2,1)} %get-tuple-element.513), channel_id=1, source_target_pairs={{64,0},{128,64},{192,128},{256,192},{320,256},{384,320},{448,384},... | collective-permute-start | bytes 196616 | tf_op jit(solution)/shard_map/while/body/eval_jaxpr/ppermute | solution.py:14
  108.6 7.8 %collective-permute-start = (bf16[4,8,8,128]{3,2,1,0:T(8,128)(2,1)}, bf16[4,8,8,128]{3,2,1,0:T(8,128)(2,1)S(1)}, u32[]{:S(2)}, u32[]{:S(2)}) collective-permute-start(bf16[4,8,8,128]{3,2,1,0:T(8,128)(2,1)} %get-tuple-element.513), channel_id=1, source_target_pairs={{64,0},{128,64},{192,128},{256,192},{320,256},{384,320},{448,384},... | collective-permute-start | bytes 196616 | tf_op jit(solution)/shard_map/while/body/eval_jaxpr/ppermute | solution.py:14
  117.1 8.8 %collective-permute-start = (bf16[4,8,8,128]{3,2,1,0:T(8,128)(2,1)}, bf16[4,8,8,128]{3,2,1,0:T(8,128)(2,1)S(1)}, u32[]{:S(2)}, u32[]{:S(2)}) collective-permute-start(bf16[4,8,8,128]{3,2,1,0:T(8,128)(2,1)} %get-tuple-element.513), channel_id=1, source_target_pairs={{64,0},{128,64},{192,128},{256,192},{320,256},{384,320},{448,384},... | collective-permute-start | bytes 196616 | tf_op jit(solution)/shard_map/while/body/eval_jaxpr/ppermute | solution.py:14
  126.5 8.8 %collective-permute-start = (bf16[4,8,8,128]{3,2,1,0:T(8,128)(2,1)}, bf16[4,8,8,128]{3,2,1,0:T(8,128)(2,1)S(1)}, u32[]{:S(2)}, u32[]{:S(2)}) collective-permute-start(bf16[4,8,8,128]{3,2,1,0:T(8,128)(2,1)} %get-tuple-element.513), channel_id=1, source_target_pairs={{64,0},{128,64},{192,128},{256,192},{320,256},{384,320},{448,384},... | collective-permute-start | bytes 196616 | tf_op jit(solution)/shard_map/while/body/eval_jaxpr/ppermute | solution.py:14
  136.0 73.2 %collective-permute-start = (bf16[4,8,8,128]{3,2,1,0:T(8,128)(2,1)}, bf16[4,8,8,128]{3,2,1,0:T(8,128)(2,1)S(1)}, u32[]{:S(2)}, u32[]{:S(2)}) collective-permute-start(bf16[4,8,8,128]{3,2,1,0:T(8,128)(2,1)} %get-tuple-element.513), channel_id=1, source_target_pairs={{64,0},{128,64},{192,128},{256,192},{320,256},{384,320},{448,384},... | collective-permute-start | bytes 196616 | tf_op jit(solution)/shard_map/while/body/eval_jaxpr/ppermute | solution.py:14
  221.1 8.8 %collective-permute-start = (bf16[4,8,8,128]{3,2,1,0:T(8,128)(2,1)}, bf16[4,8,8,128]{3,2,1,0:T(8,128)(2,1)S(1)}, u32[]{:S(2)}, u32[]{:S(2)}) collective-permute-start(bf16[4,8,8,128]{3,2,1,0:T(8,128)(2,1)} %get-tuple-element.513), channel_id=1, source_target_pairs={{64,0},{128,64},{192,128},{256,192},{320,256},{384,320},{448,384},... | collective-permute-start | bytes 196616 | tf_op jit(solution)/shard_map/while/body/eval_jaxpr/ppermute | solution.py:14
  241.9 5.2 %collective-permute-start = (bf16[4,8,8,128]{3,2,1,0:T(8,128)(2,1)}, bf16[4,8,8,128]{3,2,1,0:T(8,128)(2,1)S(1)}, u32[]{:S(2)}, u32[]{:S(2)}) collective-permute-start(bf16[4,8,8,128]{3,2,1,0:T(8,128)(2,1)} %get-tuple-element.513), channel_id=1, source_target_pairs={{64,0},{128,64},{192,128},{256,192},{320,256},{384,320},{448,384},... | collective-permute-start | bytes 196616 | tf_op jit(solution)/shard_map/while/body/eval_jaxpr/ppermute | solution.py:14
  381.1 24.9 %collective-permute-start.9 = (f32[64,128]{1,0:T(8,128)S(1)}, f32[64,128]{1,0:T(8,128)S(1)}, u32[]{:S(2)}, u32[]{:S(2)}) collective-permute-start(f32[64,128]{1,0:T(8,128)S(1)} %fusion), channel_id=1, source_target_pairs={{0,9},{1,10},{2,11},{3,12},{4,13},{5,14},{6,15},{7,16},{8,17},{9,1... | collective-permute-start | bytes 98312
  382.4 33.2 %collective-permute-start.8 = (f32[64,128]{1,0:T(8,128)S(1)}, f32[64,128]{1,0:T(8,128)S(1)}, u32[]{:S(2)}, u32[]{:S(2)}) collective-permute-start(f32[64,128]{1,0:T(8,128)S(1)} %fusion), channel_id=1, source_target_pairs={{0,8},{1,9},{2,10},{3,11},{4,12},{5,13},{6,14},{7,15},{8,16},{9,17... | collective-permute-start | bytes 98312
  383.7 33.3 %collective-permute-start.7 = (f32[64,128]{1,0:T(8,128)S(1)}, f32[64,128]{1,0:T(8,128)S(1)}, u32[]{:S(2)}, u32[]{:S(2)}) collective-permute-start(f32[64,128]{1,0:T(8,128)S(1)} %fusion), channel_id=1, source_target_pairs={{0,7},{1,8},{2,9},{3,10},{4,11},{5,12},{6,13},{7,14},{8,15},{9,16}... | collective-permute-start | bytes 98312
  385.0 35.1 %collective-permute-start.6 = (f32[64,128]{1,0:T(8,128)S(1)}, f32[64,128]{1,0:T(8,128)S(1)}, u32[]{:S(2)}, u32[]{:S(2)}) collective-permute-start(f32[64,128]{1,0:T(8,128)S(1)} %fusion), channel_id=1, source_target_pairs={{0,6},{1,7},{2,8},{3,9},{4,10},{5,11},{6,12},{7,13},{8,14},{9,15},... | collective-permute-start | bytes 98312
  396.3 7.7 %collective-permute-start.10 = (f32[54,128]{1,0:T(8,128)S(1)}, f32[54,128]{1,0:T(8,128)S(1)}, u32[]{:S(2)}, u32[]{:S(2)}) collective-permute-start(f32[54,128]{1,0:T(8,128)S(1)} %slice.604), channel_id=1, source_target_pairs={{0,10},{1,11},{2,12},{3,13},{4,14},{5,15},{6,16},{7,17},{8,18},{9,... | collective-permute-start | bytes 82952
  404.0 22.1 %collective-permute-start.5 = (f32[64,128]{1,0:T(8,128)S(1)}, f32[64,128]{1,0:T(8,128)S(1)}, u32[]{:S(2)}, u32[]{:S(2)}) collective-permute-start(f32[64,128]{1,0:T(8,128)S(1)} %fusion), channel_id=1, source_target_pairs={{0,5},{1,6},{2,7},{3,8},{4,9},{5,10},{6,11},{7,12},{8,13},{9,14},{... | collective-permute-start | bytes 98312
  406.0 20.1 %collective-permute-start.4 = (f32[64,128]{1,0:T(8,128)S(1)}, f32[64,128]{1,0:T(8,128)S(1)}, u32[]{:S(2)}, u32[]{:S(2)}) collective-permute-start(f32[64,128]{1,0:T(8,128)S(1)} %fusion), channel_id=1, source_target_pairs={{0,4},{1,5},{2,6},{3,7},{4,8},{5,9},{6,10},{7,11},{8,12},{9,13},{1... | collective-permute-start | bytes 98312
  415.6 10.4 %collective-permute-start.3 = (f32[64,128]{1,0:T(8,128)S(1)}, f32[64,128]{1,0:T(8,128)S(1)}, u32[]{:S(2)}, u32[]{:S(2)}) collective-permute-start(f32[64,128]{1,0:T(8,128)S(1)} %fusion), channel_id=1, source_target_pairs={{0,3},{1,4},{2,5},{3,6},{4,7},{5,8},{6,9},{7,10},{8,11},{9,12},{10... | collective-permute-start | bytes 98312
  416.9 9.1 %collective-permute-start.2 = (f32[64,128]{1,0:T(8,128)S(1)}, f32[64,128]{1,0:T(8,128)S(1)}, u32[]{:S(2)}, u32[]{:S(2)}) collective-permute-start(f32[64,128]{1,0:T(8,128)S(1)} %fusion), channel_id=1, source_target_pairs={{0,2},{1,3},{2,4},{3,5},{4,6},{5,7},{6,8},{7,9},{8,10},{9,11},{10,... | collective-permute-start | bytes 98312
  420.1 6.0 %collective-permute-start.1 = (f32[64,128]{1,0:T(8,128)S(1)}, f32[64,128]{1,0:T(8,128)S(1)}, u32[]{:S(2)}, u32[]{:S(2)}) collective-permute-start(f32[64,128]{1,0:T(8,128)S(1)} %fusion), channel_id=1, source_target_pairs={{0,1},{1,2},{2,3},{3,4},{4,5},{5,6},{6,7},{7,8},{8,9},{9,10},{10,1... | collective-permute-start | bytes 98312
  (47 other events, 780.0 us)
where the time goes:
time: 429 us; the launch traced here: 428 us
  blocking collectives  198 us (46%)
  waiting for transfers between devices  119 us (28%)
  starting transfers between devices  52.7 us (12%)
  matrix products  29.6 us (7%)
  local copies, waits for them, and re-layouts  20.6 us (5%)
  other arithmetic  5.32 us (1%)
    unnamed x1, blocking collectives  122 us
    ppermute x9, waiting for transfers between devices, passed_along(): return lax.ppermute(array, axis, pairs)  117 us
    all_gather x1, blocking collectives, local(): gathered = lax.all_gather(weights[0], 'dp', axis=0, tiled=True)  75.9 us
    unnamed x10, starting transfers between devices  41.2 us
    dot_general x108, matrix products, apply_taps(): jnp.dot(window_rows, kernel_taps[tap_index], preferred_element_type=jnp.f...  19.1 us
    ppermute x9, starting transfers between devices, passed_along(): return lax.ppermute(array, axis, pairs)  11.5 us
    dot_general x54, matrix products, tap_grads(): jnp.dot(window_rows.T, slope, preferred_element_type=jnp.float32)  10.4 us
  transfers between devices with their start and end apart: 19, of which 10 were waited for; matrix products, arithmetic and copies ran while one was open for 0% of the time, Pallas kernels for 0%

commit v1 on v0

--- a/solution.py
+++ b/solution.py
@@ -70,7 +70,9 @@
     segments = lax.axis_size("segment")
     dp_count = lax.axis_size("dp")
     segment_index = lax.axis_index("segment")
-    gathered = lax.all_gather(weights[0], "dp", axis=0, tiled=True)
+    gathered = jnp.concatenate(
+        lax.all_to_all(jnp.stack([weights[0]] * lax.axis_size("dp")), "dp", 0, 0), axis=0
+    )
     channels = gathered.shape[1]
     kernel_taps = gathered.reshape(-1, channels, channels)
     flipped = jnp.transpose(jnp.flip(kernel_taps, 0), (0, 2, 1))

time: 429 us -> 412 us (0.960)
  blocking collectives: 198 us -> 124 us
  waiting for transfers between devices: 119 us -> 153 us
  starting transfers between devices: 52.7 us -> 74.5 us
    all_gather x1 -> x0, blocking collectives: 75.9 us -> none  [local(): gathered = lax.all_gather(weights[0], 'dp', axis=0, tiled=True)]
    all_to_all x0 -> x1, waiting for transfers between devices: none -> 35.7 us  [local(): lax.all_to_all(jnp.stack([weights[0]] * lax.axis_size('dp')), 'dp', 0, 0)]
    all_to_all x0 -> x1, starting transfers between devices: none -> 18.2 us  [local(): lax.all_to_all(jnp.stack([weights[0]] * lax.axis_size('dp')), 'dp', 0, 0)]
  transfers between devices with their start and end apart: 19 -> 20, of which waited for: 10 -> 11; matrix products, arithmetic and copies ran while one was open for 0% -> 3% of each run, Pallas kernels for 0% -> 0%
where the time goes in v1:
time: 412 us; the launch traced here: 411 us
  waiting for transfers between devices  153 us (37%)
  blocking collectives  124 us (30%)
  starting transfers between devices  74.5 us (18%)
  matrix products  29.5 us (7%)
  local copies, waits for them, and re-layouts  20.9 us (5%)
  other arithmetic  5.31 us (1%)
    unnamed x1, blocking collectives  124 us
    ppermute x9, waiting for transfers between devices, passed_along(): return lax.ppermute(array, axis, pairs)  116 us
    unnamed x10, starting transfers between devices  44.8 us
    all_to_all x1, waiting for transfers between devices, local(): lax.all_to_all(jnp.stack([weights[0]] * lax.axis_size('dp')), 'dp', 0, 0)  35.7 us
    dot_general x108, matrix products, apply_taps(): jnp.dot(window_rows, kernel_taps[tap_index], preferred_element_type=jnp.f...  19.1 us
    all_to_all x1, starting transfers between devices, local(): lax.all_to_all(jnp.stack([weights[0]] * lax.axis_size('dp')), 'dp', 0, 0)  18.2 us
    ppermute x9, starting transfers between devices, passed_along(): return lax.ppermute(array, axis, pairs)  11.5 us
    dot_general x54, matrix products, tap_grads(): jnp.dot(window_rows.T, slope, preferred_element_type=jnp.float32)  10.4 us
  transfers between devices with their start and end apart: 20, of which 11 were waited for; matrix products, arithmetic and copies ran while one was open for 3% of the time, Pallas kernels for 0%

profile of v1, /device:TPU:1, one launch (start us, length us, event | category | flops | bytes accessed | tf_op | source)
XLA Modules:
  0.0 410.8 jit_solution(506353003627990430)
XLA Ops:
  0.7 1.8 stack.6
  2.5 18.2 %all-to-all-start = ((bf16[64,54,128]{2,1,0:T(8,128)(2,1)}), bf16[64,54,128]{2,1,0:T(8,128)(2,1)S(1)}, u32[]{:S(2)}, u32[]{:S(2)}) async-start(bf16[64,54,128]{2,1,0:T(8,128)(2,1)} %stack.6), calls=%async_computation | async-start | bytes 1835008 | tf_op jit(solution)/shard_map/all_to_all | solution.py:74
  30.3 35.7 %all-to-all-done = bf16[64,54,128]{2,1,0:T(8,128)(2,1)S(1)} async-done(((bf16[64,54,128]{2,1,0:T(8,128)(2,1)}), bf16[64,54,128]{2,1,0:T(8,128)(2,1)S(1)}, u32[]{:S(2)}, u32[]{:S(2)}) %all-to-all-start) | async-done | bytes 884768 | tf_op jit(solution)/shard_map/all_to_all | solution.py:74
  68.5 156.3 %while.18 = (s32[]{:T(128)}, bf16[4,8,8,128]{3,2,1,0:T(8,128)(2,1)S(1)}, bf16[2,4,8,8,128]{4,3,2,1,0:T(8,128)(2,1)}, bf16[2,256,128]{2,1,0:T(8,128)(2,1)S(1)}, s...) while((s32[]{:T(128)}, ...), condition=%wide.region_3.4_spmd, body=%wide.region_0.3_spmd.sunk | while | flops 455180288 | bytes 23921024 | solution.py:136
  70.4 3.9 collective-permute-done
  76.3 3.9 collective-permute-done
  82.1 3.9 collective-permute-done
  87.9 6.5 %collective-permute-done = bf16[4,8,8,128]{3,2,1,0:T(8,128)(2,1)S(1)} collective-permute-done((bf16[4,8,8,128]{3,2,1,0:T(8,128)(2,1)}, bf16[4,8,8,128]{3,2,1,0:T(8,128)(2,1)S(1)}, u32[]{:S(2)}, u32[]{:S(2)}) %collective-permute-start) | collective-permute-done | bytes 65568 | tf_op jit(solution)/shard_map/while/body/eval_jaxpr/ppermute | solution.py:14
  96.4 7.5 %collective-permute-done = bf16[4,8,8,128]{3,2,1,0:T(8,128)(2,1)S(1)} collective-permute-done((bf16[4,8,8,128]{3,2,1,0:T(8,128)(2,1)}, bf16[4,8,8,128]{3,2,1,0:T(8,128)(2,1)S(1)}, u32[]{:S(2)}, u32[]{:S(2)}) %collective-permute-start) | collective-permute-done | bytes 65568 | tf_op jit(solution)/shard_map/while/body/eval_jaxpr/ppermute | solution.py:14
  105.8 7.5 %collective-permute-done = bf16[4,8,8,128]{3,2,1,0:T(8,128)(2,1)S(1)} collective-permute-done((bf16[4,8,8,128]{3,2,1,0:T(8,128)(2,1)}, bf16[4,8,8,128]{3,2,1,0:T(8,128)(2,1)S(1)}, u32[]{:S(2)}, u32[]{:S(2)}) %collective-permute-start) | collective-permute-done | bytes 65568 | tf_op jit(solution)/shard_map/while/body/eval_jaxpr/ppermute | solution.py:14
  115.3 71.6 %collective-permute-done = bf16[4,8,8,128]{3,2,1,0:T(8,128)(2,1)S(1)} collective-permute-done((bf16[4,8,8,128]{3,2,1,0:T(8,128)(2,1)}, bf16[4,8,8,128]{3,2,1,0:T(8,128)(2,1)S(1)}, u32[]{:S(2)}, u32[]{:S(2)}) %collective-permute-start) | collective-permute-done | bytes 65568 | tf_op jit(solution)/shard_map/while/body/eval_jaxpr/ppermute | solution.py:14
  186.9 11.9 %conditional.2 = (bf16[4,8,8,128]{3,2,1,0:T(8,128)(2,1)}, bf16[2,4,8,8,128]{4,3,2,1,0:T(8,128)(2,1)}, bf16[2,256,128]{2,1,0:T(8,128)(2,1)S(1)}) conditional(s32[]{:T(128)} %convert_element_type.107, (bf16[2,4,8,8,128]{4,3,2,1,0:T(8,128)(2,1)}, bf16[2,256,128]{2,1,0:T(8,128)(2,1)S(1)}) %tuple.171, (s32[]{:T(128)}, s32[]{:T(128)}, ...), branch_computations={%region_1.1_spmd, %region_2.2_spmd} | conditional | flops 455180288 | bytes 23658574 | solution.py:124
  197.3 1.5 constant_dynamic-update-slice_fusion
  200.1 7.5 %collective-permute-done = bf16[4,8,8,128]{3,2,1,0:T(8,128)(2,1)S(1)} collective-permute-done((bf16[4,8,8,128]{3,2,1,0:T(8,128)(2,1)}, bf16[4,8,8,128]{3,2,1,0:T(8,128)(2,1)S(1)}, u32[]{:S(2)}, u32[]{:S(2)}) %collective-permute-start) | collective-permute-done | bytes 65568 | tf_op jit(solution)/shard_map/while/body/eval_jaxpr/ppermute | solution.py:14
  207.6 11.9 %conditional.2 = (bf16[4,8,8,128]{3,2,1,0:T(8,128)(2,1)}, bf16[2,4,8,8,128]{4,3,2,1,0:T(8,128)(2,1)}, bf16[2,256,128]{2,1,0:T(8,128)(2,1)S(1)}) conditional(s32[]{:T(128)} %convert_element_type.107, (bf16[2,4,8,8,128]{4,3,2,1,0:T(8,128)(2,1)}, bf16[2,256,128]{2,1,0:T(8,128)(2,1)S(1)}) %tuple.171, (s32[]{:T(128)}, s32[]{:T(128)}, ...), branch_computations={%region_1.1_spmd, %region_2.2_spmd} | conditional | flops 455180288 | bytes 23658574 | solution.py:124
  220.8 3.9 collective-permute-done
  236.4 124.2 %fusion = f32[64,128]{1,0:T(8,128)S(1)} fusion(f32[3456,128]{1,0:T(8,128)S(1)} %add.436), kind=kCustom, calls=%all-reduce-scatter | all-reduce-scatter fusion | flops 524289 | bytes 1804288
  364.6 14.2 %collective-permute-start.6 = (f32[64,128]{1,0:T(8,128)S(1)}, f32[64,128]{1,0:T(8,128)S(1)}, u32[]{:S(2)}, u32[]{:S(2)}) collective-permute-start(f32[64,128]{1,0:T(8,128)S(1)} %fusion), channel_id=1, source_target_pairs={{0,6},{1,7},{2,8},{3,9},{4,10},{5,11},{6,12},{7,13},{8,14},{9,15},... | collective-permute-start | bytes 98312
  378.8 6.0 %collective-permute-start.10 = (f32[54,128]{1,0:T(8,128)S(1)}, f32[54,128]{1,0:T(8,128)S(1)}, u32[]{:S(2)}, u32[]{:S(2)}) collective-permute-start(f32[54,128]{1,0:T(8,128)S(1)} %slice.604), channel_id=1, source_target_pairs={{0,10},{1,11},{2,12},{3,13},{4,14},{5,15},{6,16},{7,17},{8,18},{9,... | collective-permute-start | bytes 82952
  385.8 3.2 collective-permute-start.5
  389.0 8.8 %collective-permute-start.4 = (f32[64,128]{1,0:T(8,128)S(1)}, f32[64,128]{1,0:T(8,128)S(1)}, u32[]{:S(2)}, u32[]{:S(2)}) collective-permute-start(f32[64,128]{1,0:T(8,128)S(1)} %fusion), channel_id=1, source_target_pairs={{0,4},{1,5},{2,6},{3,7},{4,8},{5,9},{6,10},{7,11},{8,12},{9,13},{1... | collective-permute-start | bytes 98312
  399.1 3.1 collective-permute-start.2
  402.3 4.2 %collective-permute-start.1 = (f32[64,128]{1,0:T(8,128)S(1)}, f32[64,128]{1,0:T(8,128)S(1)}, u32[]{:S(2)}, u32[]{:S(2)}) collective-permute-start(f32[64,128]{1,0:T(8,128)S(1)} %fusion), channel_id=1, source_target_pairs={{0,1},{1,2},{2,3},{3,4},{4,5},{5,6},{6,7},{7,8},{8,9},{9,10},{10,1... | collective-permute-start | bytes 98312
  408.4 1.7 concatenate.8
  (345 shorter events, 72.9 us)
Async XLA Ops:
  2.5 63.5 %all-to-all-start = ((bf16[64,54,128]{2,1,0:T(8,128)(2,1)}), bf16[64,54,128]{2,1,0:T(8,128)(2,1)S(1)}, u32[]{:S(2)}, u32[]{:S(2)}) async-start(bf16[64,54,128]{2,1,0:T(8,128)(2,1)} %stack.6), calls=%async_computation | async-start | bytes 1835008 | tf_op jit(solution)/shard_map/all_to_all | solution.py:74
  68.5 157.4 %copy-start.43 = (bf16[4,8,8,128]{3,2,1,0:T(8,128)(2,1)S(1)}, bf16[4,8,8,128]{3,2,1,0:T(8,128)(2,1)}, u32[]{:S(2)}) copy-start(bf16[4,8,8,128]{3,2,1,0:T(8,128)(2,1)} %get-tuple-element.406) | copy-start | bytes 196612
  68.5 157.6 %copy-start.42 = (bf16[4,8,8,128]{3,2,1,0:T(8,128)(2,1)S(1)}, bf16[4,8,8,128]{3,2,1,0:T(8,128)(2,1)}, u32[]{:S(2)}) copy-start(bf16[4,8,8,128]{3,2,1,0:T(8,128)(2,1)} %get-tuple-element.407) | copy-start | bytes 196612
  68.5 157.8 %copy-start.41 = (bf16[4,8,8,128]{3,2,1,0:T(8,128)(2,1)S(1)}, bf16[4,8,8,128]{3,2,1,0:T(8,128)(2,1)}, u32[]{:S(2)}) copy-start(bf16[4,8,8,128]{3,2,1,0:T(8,128)(2,1)} %get-tuple-element.408) | copy-start | bytes 196612
  68.5 158.1 %copy-start.39 = (bf16[4,8,8,128]{3,2,1,0:T(8,128)(2,1)S(1)}, bf16[4,8,8,128]{3,2,1,0:T(8,128)(2,1)}, u32[]{:S(2)}) copy-start(bf16[4,8,8,128]{3,2,1,0:T(8,128)(2,1)} %get-tuple-element.409) | copy-start | bytes 196612
  69.2 5.2 %collective-permute-start = (bf16[4,8,8,128]{3,2,1,0:T(8,128)(2,1)}, bf16[4,8,8,128]{3,2,1,0:T(8,128)(2,1)S(1)}, u32[]{:S(2)}, u32[]{:S(2)}) collective-permute-start(bf16[4,8,8,128]{3,2,1,0:T(8,128)(2,1)} %get-tuple-element.524), channel_id=1, source_target_pairs={{64,0},{128,64},{192,128},{256,192},{320,256},{384,320},{448,384},... | collective-permute-start | bytes 196616 | tf_op jit(solution)/shard_map/while/body/eval_jaxpr/ppermute | solution.py:14
  75.0 5.2 %collective-permute-start = (bf16[4,8,8,128]{3,2,1,0:T(8,128)(2,1)}, bf16[4,8,8,128]{3,2,1,0:T(8,128)(2,1)S(1)}, u32[]{:S(2)}, u32[]{:S(2)}) collective-permute-start(bf16[4,8,8,128]{3,2,1,0:T(8,128)(2,1)} %get-tuple-element.524), channel_id=1, source_target_pairs={{64,0},{128,64},{192,128},{256,192},{320,256},{384,320},{448,384},... | collective-permute-start | bytes 196616 | tf_op jit(solution)/shard_map/while/body/eval_jaxpr/ppermute | solution.py:14
  80.8 5.2 %collective-permute-start = (bf16[4,8,8,128]{3,2,1,0:T(8,128)(2,1)}, bf16[4,8,8,128]{3,2,1,0:T(8,128)(2,1)S(1)}, u32[]{:S(2)}, u32[]{:S(2)}) collective-permute-start(bf16[4,8,8,128]{3,2,1,0:T(8,128)(2,1)} %get-tuple-element.524), channel_id=1, source_target_pairs={{64,0},{128,64},{192,128},{256,192},{320,256},{384,320},{448,384},... | collective-permute-start | bytes 196616 | tf_op jit(solution)/shard_map/while/body/eval_jaxpr/ppermute | solution.py:14
  86.6 7.8 %collective-permute-start = (bf16[4,8,8,128]{3,2,1,0:T(8,128)(2,1)}, bf16[4,8,8,128]{3,2,1,0:T(8,128)(2,1)S(1)}, u32[]{:S(2)}, u32[]{:S(2)}) collective-permute-start(bf16[4,8,8,128]{3,2,1,0:T(8,128)(2,1)} %get-tuple-element.524), channel_id=1, source_target_pairs={{64,0},{128,64},{192,128},{256,192},{320,256},{384,320},{448,384},... | collective-permute-start | bytes 196616 | tf_op jit(solution)/shard_map/while/body/eval_jaxpr/ppermute | solution.py:14
  95.1 8.8 %collective-permute-start = (bf16[4,8,8,128]{3,2,1,0:T(8,128)(2,1)}, bf16[4,8,8,128]{3,2,1,0:T(8,128)(2,1)S(1)}, u32[]{:S(2)}, u32[]{:S(2)}) collective-permute-start(bf16[4,8,8,128]{3,2,1,0:T(8,128)(2,1)} %get-tuple-element.524), channel_id=1, source_target_pairs={{64,0},{128,64},{192,128},{256,192},{320,256},{384,320},{448,384},... | collective-permute-start | bytes 196616 | tf_op jit(solution)/shard_map/while/body/eval_jaxpr/ppermute | solution.py:14
  104.5 8.8 %collective-permute-start = (bf16[4,8,8,128]{3,2,1,0:T(8,128)(2,1)}, bf16[4,8,8,128]{3,2,1,0:T(8,128)(2,1)S(1)}, u32[]{:S(2)}, u32[]{:S(2)}) collective-permute-start(bf16[4,8,8,128]{3,2,1,0:T(8,128)(2,1)} %get-tuple-element.524), channel_id=1, source_target_pairs={{64,0},{128,64},{192,128},{256,192},{320,256},{384,320},{448,384},... | collective-permute-start | bytes 196616 | tf_op jit(solution)/shard_map/while/body/eval_jaxpr/ppermute | solution.py:14
  114.0 72.9 %collective-permute-start = (bf16[4,8,8,128]{3,2,1,0:T(8,128)(2,1)}, bf16[4,8,8,128]{3,2,1,0:T(8,128)(2,1)S(1)}, u32[]{:S(2)}, u32[]{:S(2)}) collective-permute-start(bf16[4,8,8,128]{3,2,1,0:T(8,128)(2,1)} %get-tuple-element.524), channel_id=1, source_target_pairs={{64,0},{128,64},{192,128},{256,192},{320,256},{384,320},{448,384},... | collective-permute-start | bytes 196616 | tf_op jit(solution)/shard_map/while/body/eval_jaxpr/ppermute | solution.py:14
  198.8 8.8 %collective-permute-start = (bf16[4,8,8,128]{3,2,1,0:T(8,128)(2,1)}, bf16[4,8,8,128]{3,2,1,0:T(8,128)(2,1)S(1)}, u32[]{:S(2)}, u32[]{:S(2)}) collective-permute-start(bf16[4,8,8,128]{3,2,1,0:T(8,128)(2,1)} %get-tuple-element.524), channel_id=1, source_target_pairs={{64,0},{128,64},{192,128},{256,192},{320,256},{384,320},{448,384},... | collective-permute-start | bytes 196616 | tf_op jit(solution)/shard_map/while/body/eval_jaxpr/ppermute | solution.py:14
  219.5 5.2 %collective-permute-start = (bf16[4,8,8,128]{3,2,1,0:T(8,128)(2,1)}, bf16[4,8,8,128]{3,2,1,0:T(8,128)(2,1)S(1)}, u32[]{:S(2)}, u32[]{:S(2)}) collective-permute-start(bf16[4,8,8,128]{3,2,1,0:T(8,128)(2,1)} %get-tuple-element.524), channel_id=1, source_target_pairs={{64,0},{128,64},{192,128},{256,192},{320,256},{384,320},{448,384},... | collective-permute-start | bytes 196616 | tf_op jit(solution)/shard_map/while/body/eval_jaxpr/ppermute | solution.py:14
  360.6 28.4 %collective-permute-start.9 = (f32[64,128]{1,0:T(8,128)S(1)}, f32[64,128]{1,0:T(8,128)S(1)}, u32[]{:S(2)}, u32[]{:S(2)}) collective-permute-start(f32[64,128]{1,0:T(8,128)S(1)} %fusion), channel_id=1, source_target_pairs={{0,9},{1,10},{2,11},{3,12},{4,13},{5,14},{6,15},{7,16},{8,17},{9,1... | collective-permute-start | bytes 98312
  361.9 36.0 %collective-permute-start.8 = (f32[64,128]{1,0:T(8,128)S(1)}, f32[64,128]{1,0:T(8,128)S(1)}, u32[]{:S(2)}, u32[]{:S(2)}) collective-permute-start(f32[64,128]{1,0:T(8,128)S(1)} %fusion), channel_id=1, source_target_pairs={{0,8},{1,9},{2,10},{3,11},{4,12},{5,13},{6,14},{7,15},{8,16},{9,17... | collective-permute-start | bytes 98312
  363.2 36.0 %collective-permute-start.7 = (f32[64,128]{1,0:T(8,128)S(1)}, f32[64,128]{1,0:T(8,128)S(1)}, u32[]{:S(2)}, u32[]{:S(2)}) collective-permute-start(f32[64,128]{1,0:T(8,128)S(1)} %fusion), channel_id=1, source_target_pairs={{0,7},{1,8},{2,9},{3,10},{4,11},{5,12},{6,13},{7,14},{8,15},{9,16}... | collective-permute-start | bytes 98312
  364.6 37.7 %collective-permute-start.6 = (f32[64,128]{1,0:T(8,128)S(1)}, f32[64,128]{1,0:T(8,128)S(1)}, u32[]{:S(2)}, u32[]{:S(2)}) collective-permute-start(f32[64,128]{1,0:T(8,128)S(1)} %fusion), channel_id=1, source_target_pairs={{0,6},{1,7},{2,8},{3,9},{4,10},{5,11},{6,12},{7,13},{8,14},{9,15},... | collective-permute-start | bytes 98312
  378.8 6.9 %collective-permute-start.10 = (f32[54,128]{1,0:T(8,128)S(1)}, f32[54,128]{1,0:T(8,128)S(1)}, u32[]{:S(2)}, u32[]{:S(2)}) collective-permute-start(f32[54,128]{1,0:T(8,128)S(1)} %slice.604), channel_id=1, source_target_pairs={{0,10},{1,11},{2,12},{3,13},{4,14},{5,15},{6,16},{7,17},{8,18},{9,... | collective-permute-start | bytes 82952
  385.8 22.6 %collective-permute-start.5 = (f32[64,128]{1,0:T(8,128)S(1)}, f32[64,128]{1,0:T(8,128)S(1)}, u32[]{:S(2)}, u32[]{:S(2)}) collective-permute-start(f32[64,128]{1,0:T(8,128)S(1)} %fusion), channel_id=1, source_target_pairs={{0,5},{1,6},{2,7},{3,8},{4,9},{5,10},{6,11},{7,12},{8,13},{9,14},{... | collective-permute-start | bytes 98312
  389.0 19.4 %collective-permute-start.4 = (f32[64,128]{1,0:T(8,128)S(1)}, f32[64,128]{1,0:T(8,128)S(1)}, u32[]{:S(2)}, u32[]{:S(2)}) collective-permute-start(f32[64,128]{1,0:T(8,128)S(1)} %fusion), channel_id=1, source_target_pairs={{0,4},{1,5},{2,6},{3,7},{4,8},{5,9},{6,10},{7,11},{8,12},{9,13},{1... | collective-permute-start | bytes 98312
  397.8 10.6 %collective-permute-start.3 = (f32[64,128]{1,0:T(8,128)S(1)}, f32[64,128]{1,0:T(8,128)S(1)}, u32[]{:S(2)}, u32[]{:S(2)}) collective-permute-start(f32[64,128]{1,0:T(8,128)S(1)} %fusion), channel_id=1, source_target_pairs={{0,3},{1,4},{2,5},{3,6},{4,7},{5,8},{6,9},{7,10},{8,11},{9,12},{10... | collective-permute-start | bytes 98312
  399.1 9.3 %collective-permute-start.2 = (f32[64,128]{1,0:T(8,128)S(1)}, f32[64,128]{1,0:T(8,128)S(1)}, u32[]{:S(2)}, u32[]{:S(2)}) collective-permute-start(f32[64,128]{1,0:T(8,128)S(1)} %fusion), channel_id=1, source_target_pairs={{0,2},{1,3},{2,4},{3,5},{4,6},{5,7},{6,8},{7,9},{8,10},{9,11},{10,... | collective-permute-start | bytes 98312
  402.3 6.1 %collective-permute-start.1 = (f32[64,128]{1,0:T(8,128)S(1)}, f32[64,128]{1,0:T(8,128)S(1)}, u32[]{:S(2)}, u32[]{:S(2)}) collective-permute-start(f32[64,128]{1,0:T(8,128)S(1)} %fusion), channel_id=1, source_target_pairs={{0,1},{1,2},{2,3},{3,4},{4,5},{5,6},{6,7},{7,8},{8,9},{9,10},{10,1... | collective-permute-start | bytes 98312
  (47 other events, 993.6 us)
